TPU v7x, 256 devices: a whole 4x4x8 slice. The times are simulated.
256 devices in a mesh: node: 32 (over y, x, z_lo), shot: 8 (over z_hi, core).
Axes of the slice: x: 4, y: 4, z: 8 (z_hi: 4, z_lo: 2; z = z_hi * 2 + z_lo), core: 2. Of those that a mesh axis runs over, the one named last changes fastest.
Arguments:
- spectra: bfloat16 [64, 2, 1024, 4096], P(None, None, 'shot', 'node'), may hold values from -6 to 6
- source_block: int32 [6], replicated, may hold values from 0 to 127
- taper_window: int32 [6, 1024], replicated, may hold values from 0 to 7
Outputs:
- virtual_gathers: bfloat16 [6, 64, 2, 32, 4096], P(None, 'shot', None, None, 'node')
All inputs are finite; a program needn't handle non-finite values.
Results may differ from a plain program's by a relative error of at most 0.0047.
Values may be sent and summed in bfloat16 or wider, within the bound.
No kernel may reach another device: no remote copies, remote signals or barrier semaphores. Data moves between devices by JAX's collectives and lax.ppermute only.
A program may use at most 128 MiB of HBM per device.

v0:
```python
import jax
import jax.numpy as jnp
import numpy as np
from jax import lax
from jax.sharding import Mesh, PartitionSpec as P

SB = 32
ROUNDS = 6
WINDOWS = 8
CHUNKS = 2
PLANE = ("y", "x")


def taper_weights(taper_windows):
    return 0.5 - 0.5 * jnp.cos(jnp.pi * (taper_windows.astype(jnp.float32) + 1.0) / (WINDOWS + 1.0))


def pick_sources(spectra, source_block):
    node_dev = spectra.shape[3]
    per_device = node_dev // SB
    me = (lax.axis_index("y") * lax.axis_size("x") + lax.axis_index("x")) * lax.axis_size(
        "zl"
    ) + lax.axis_index("zl")
    owner = source_block // per_device
    first = source_block % per_device * SB
    column = jnp.arange(ROUNDS * SB, dtype=jnp.int32)
    wanted = first[column // SB] + column % SB
    keep = owner[column // SB] == me
    node = jnp.arange(node_dev, dtype=jnp.int32)
    select = ((node[:, None] == wanted[None, :]) & keep[None, :]).astype(spectra.dtype)
    select = select.reshape(node_dev, CHUNKS, ROUNDS * SB // CHUNKS)
    picked = jnp.einsum("fckn,nhq->hfcqk", spectra, select, preferred_element_type=jnp.float32)
    return picked.astype(spectra.dtype)


def broadcast(piece, pending=None):
    part = lax.psum_scatter(piece, PLANE, scatter_dimension=0, tiled=True)
    other = lax.ppermute(part, "zl", perm=[(0, 1), (1, 0)])
    part = part + other
    if pending is not None:
        part, pending = lax.optimization_barrier((part, pending))
    return (lax.all_gather(part, PLANE, axis=0, tiled=True), pending)


def shot_reduce(partial):
    nz = lax.axis_size("zh")
    nc = lax.axis_size("c")
    zh = lax.axis_index("zh")
    c = lax.axis_index("c")
    freqs = partial.shape[0]
    grouped = partial.reshape(nz, nc, freqs // (nz * nc), *partial.shape[1:])
    send = lax.dynamic_index_in_dim(grouped, 1 - c, axis=1, keepdims=False)
    keep = lax.dynamic_index_in_dim(grouped, c, axis=1, keepdims=False)
    mine = keep + lax.ppermute(send, "c", perm=[(0, 1), (1, 0)])
    half = mine.shape[-1] // 2
    forward = mine[..., :half]
    backward = mine[..., half:]
    up = [(j, (j + 1) % nz) for j in range(nz)]
    down = [(j, (j - 1) % nz) for j in range(nz)]
    acc_f = lax.dynamic_index_in_dim(forward, (zh - 1) % nz, axis=0, keepdims=False)
    acc_b = lax.dynamic_index_in_dim(backward, (zh + 1) % nz, axis=0, keepdims=False)
    for step in range(nz - 1):
        got_f = lax.ppermute(acc_f, "zh", perm=up)
        got_b = lax.ppermute(acc_b, "zh", perm=down)
        acc_f = got_f + lax.dynamic_index_in_dim(
            forward, (zh - 2 - step) % nz, axis=0, keepdims=False
        )
        acc_b = got_b + lax.dynamic_index_in_dim(
            backward, (zh + 2 + step) % nz, axis=0, keepdims=False
        )
    return jnp.concatenate((acc_f, acc_b), axis=-1)


def body(spectra, source_block, taper_window):
    freqs, _, shot_dev, node_dev = spectra.shape
    shot_groups = lax.axis_size("zh") * lax.axis_size("c")
    scale = 1.0 / jnp.sqrt(jnp.float32(shot_dev * shot_groups))
    shot_weights = taper_weights(taper_window)
    shot_index = lax.axis_index("zh") * lax.axis_size("c") + lax.axis_index("c")
    local_weights = lax.dynamic_slice_in_dim(shot_weights, shot_index * shot_dev, shot_dev, 1)
    weight_rows = jnp.repeat(local_weights, SB, axis=0).reshape(CHUNKS, -1, shot_dev)
    receivers = spectra.reshape(freqs, 2 * shot_dev, node_dev)
    picked = pick_sources(spectra, source_block)
    results = []
    summed = None
    for chunk in range(CHUNKS):
        piece = picked[chunk]
        pending = None
        if summed is not None:
            piece, summed = lax.optimization_barrier((piece, summed))
            pending = shot_reduce(summed * scale)
        source, pending = broadcast(piece, pending)
        if pending is not None:
            results.append(pending)
        tapered = (source.astype(jnp.float32) * weight_rows[chunk][None, None]).astype(jnp.bfloat16)
        real_part = tapered[:, 0]
        imag_part = tapered[:, 1]
        real_row = jnp.concatenate((real_part, imag_part), axis=2)
        imag_row = jnp.concatenate((-imag_part, real_part), axis=2)
        operator = jnp.stack((real_row, imag_row), axis=1)
        summed = jnp.einsum(
            "foqK,fKn->foqn", operator, receivers, preferred_element_type=jnp.float32
        )
    results.append(shot_reduce(summed * scale))
    reduced = jnp.concatenate(results, axis=2)
    local_f = reduced.shape[0]
    reduced = reduced.reshape(local_f, 2, ROUNDS, SB, node_dev)
    return jnp.transpose(reduced, (2, 0, 1, 3, 4)).astype(jnp.bfloat16)


def solution(mesh):
    devices = np.asarray(mesh.devices).reshape(4, 4, 2, 4, 2)
    fine = Mesh(devices, ("y", "x", "zl", "zh", "c"))
    in_specs = (P(None, None, ("zh", "c"), ("y", "x", "zl")), P(), P())
    out_specs = P(None, ("zh", "c"), None, None, ("y", "x", "zl"))
    return jax.shard_map(body, mesh=fine, in_specs=in_specs, out_specs=out_specs, check_vma=False)
```

profile of v0, /device:TPU:1, one launch (start us, length us, event | category | flops | bytes accessed | tf_op | source)
XLA Modules:
  0.0 471.3 jit_solution(1348825625948598850)
XLA Ops:
  7.9 3.7 fusion.28
  11.7 3.8 compare_reduce_fusion
  15.6 4.0 convert_bitcast_fusion
  19.6 3.9 slice_bitcast_fusion
  23.5 82.9 %reduce-scatter.3.cloned.1.call-done = bf16[4,2,96,128]{3,2,1,0:T(8,128)(2,1)} async-done(((bf16[64,2,96,128]{3,2,1,0:T(8,128)(2,1)}), bf16[4,2,96,128]{3,2,1,0:T(8,128)(2,1)}) %reduce-scatter.3.cloned.1.call-update) | async-done | bytes 196624 | tf_op jit(solution)/shard_map/reduce_scatter | solution.py:37
  107.8 3.4 collective-permute-done
  113.7 54.2 %all-gather.3.cloned.1.call-done = bf16[64,2,96,128]{3,2,1,0:T(8,128)(2,1)} async-done(((bf16[4,2,96,128]{3,2,1,0:T(8,128)(2,1)}), bf16[64,2,96,128]{3,2,1,0:T(8,128)(2,1)}) %all-gather.3.cloned.1.call-update) | async-done | bytes 3145744 | tf_op jit(solution)/shard_map/all_gather | solution.py:42
  167.9 2.5 multiply_convert_fusion.1
  173.0 3.6 fusion
  176.6 3.4 broadcast_multiply_fusion.1
  180.3 2.4 copy-done
  183.8 5.3 %collective-permute-done.2 = f32[4,8,2,96,128]{4,3,2,1,0:T(8,128)} collective-permute-done((f32[4,8,2,96,128]{4,3,2,1,0:T(8,128)S(1)}, f32[4,8,2,96,128]{4,3,2,1,0:T(8,128)}, u32[]{:S(2)}, u32[]{:S(2)}) %collective-permute-start.2) | collective-permute-done | bytes 3145760 | tf_op jit(solution)/shard_map/ppermute | solution.py:54
  189.1 3.4 bitcast_add_fusion.1
  196.8 2.2 copy.19
  199.0 3.8 collective-permute-start.6
  204.3 2.2 copy.15
  206.5 2.2 copy.20
  208.7 2.2 copy.16
  210.9 20.5 %collective-permute-done.6 = f32[8,2,96,64]{2,3,1,0:T(8,128)} collective-permute-done((f32[8,2,96,64]{2,3,1,0:T(8,128)}, f32[8,2,96,64]{2,3,1,0:T(8,128)}, u32[]{:S(2)}, u32[]{:S(2)}) %collective-permute-start.6) | collective-permute-done | bytes 393248 | tf_op jit(solution)/shard_map/ppermute | solution.py:64
  233.5 4.5 collective-permute-start.7
  240.0 2.2 copy.21
  242.2 2.2 copy.17
  244.4 6.8 %collective-permute-done.7 = f32[8,2,96,64]{2,3,1,0:T(8,128)} collective-permute-done((f32[8,2,96,64]{2,3,1,0:T(8,128)}, f32[8,2,96,64]{2,3,1,0:T(8,128)}, u32[]{:S(2)}, u32[]{:S(2)}) %collective-permute-start.7) | collective-permute-done | bytes 393248 | tf_op jit(solution)/shard_map/ppermute | solution.py:64
  253.3 2.7 collective-permute-start.8
  256.0 5.8 %collective-permute-done.4 = f32[8,2,96,64]{2,3,1,0:T(8,128)} collective-permute-done((f32[8,2,96,64]{2,3,1,0:T(8,128)}, f32[8,2,96,64]{2,3,1,0:T(8,128)}, u32[]{:S(2)}, u32[]{:S(2)}) %collective-permute-start.4) | collective-permute-done | bytes 393248 | tf_op jit(solution)/shard_map/ppermute | solution.py:63
  266.0 9.4 %collective-permute-done.8 = f32[8,2,96,64]{2,3,1,0:T(8,128)} collective-permute-done((f32[8,2,96,64]{2,3,1,0:T(8,128)}, f32[8,2,96,64]{2,3,1,0:T(8,128)}, u32[]{:S(2)}, u32[]{:S(2)}) %collective-permute-start.8) | collective-permute-done | bytes 393248 | tf_op jit(solution)/shard_map/ppermute | solution.py:64
  275.4 2.2 copy.22
  277.6 7.9 %collective-permute-done.5 = f32[8,2,96,64]{2,3,1,0:T(8,128)} collective-permute-done((f32[8,2,96,64]{2,3,1,0:T(8,128)}, f32[8,2,96,64]{2,3,1,0:T(8,128)}, u32[]{:S(2)}, u32[]{:S(2)}) %collective-permute-start.5) | collective-permute-done | bytes 393248 | tf_op jit(solution)/shard_map/ppermute | solution.py:63
  285.5 2.2 copy.18
  291.5 2.5 collective-permute-done.1
  294.7 55.8 %all-gather.5.cloned.1.call-done = bf16[64,2,96,128]{3,2,1,0:T(8,128)(2,1)} async-done(((bf16[4,2,96,128]{3,2,1,0:T(8,128)(2,1)}), bf16[64,2,96,128]{3,2,1,0:T(8,128)(2,1)}) %all-gather.5.cloned.1.call-update) | async-done | bytes 3145744 | tf_op jit(solution)/shard_map/all_gather | solution.py:42
  350.5 2.5 multiply_convert_fusion
  358.9 5.3 %collective-permute-done.9 = f32[4,8,2,96,128]{4,3,2,1,0:T(8,128)S(1)} collective-permute-done((f32[4,8,2,96,128]{4,3,2,1,0:T(8,128)S(1)}, f32[4,8,2,96,128]{4,3,2,1,0:T(8,128)S(1)}, u32[]{:S(2)}, u32[]{:S(2)}) %collective-permute-start.9) | collective-permute-done | bytes 3145760 | tf_op jit(solution)/shard_map/ppermute | solution.py:54
  369.0 2.2 copy.29
  371.2 3.8 collective-permute-start.13
  378.7 2.2 copy.30
  380.9 22.7 %collective-permute-done.13 = f32[8,2,96,64]{2,3,1,0:T(8,128)} collective-permute-done((f32[8,2,96,64]{2,3,1,0:T(8,128)}, f32[8,2,96,64]{2,3,1,0:T(8,128)}, u32[]{:S(2)}, u32[]{:S(2)}) %collective-permute-start.13) | collective-permute-done | bytes 393248 | tf_op jit(solution)/shard_map/ppermute | solution.py:64
  405.7 4.5 collective-permute-start.14
  410.2 2.2 copy.26
  416.7 2.2 copy.27
  418.9 4.6 collective-permute-done.14
  424.7 2.8 collective-permute-start.15
  427.5 6.6 %collective-permute-done.11 = f32[8,2,96,64]{2,3,1,0:T(8,128)} collective-permute-done((f32[8,2,96,64]{2,3,1,0:T(8,128)}, f32[8,2,96,64]{2,3,1,0:T(8,128)}, u32[]{:S(2)}, u32[]{:S(2)}) %collective-permute-start.11) | collective-permute-done | bytes 393248 | tf_op jit(solution)/shard_map/ppermute | solution.py:63
  438.2 9.4 %collective-permute-done.15 = f32[8,2,96,64]{2,3,1,0:T(8,128)} collective-permute-done((f32[8,2,96,64]{2,3,1,0:T(8,128)S(1)}, f32[8,2,96,64]{2,3,1,0:T(8,128)}, u32[]{:S(2)}, u32[]{:S(2)}) %collective-permute-start.15) | collective-permute-done | bytes 393248 | tf_op jit(solution)/shard_map/ppermute | solution.py:64
  447.6 2.2 copy.32
  449.8 2.2 fusion.14
  452.0 7.0 %collective-permute-done.12 = f32[8,2,96,64]{2,3,1,0:T(8,128)} collective-permute-done((f32[8,2,96,64]{2,3,1,0:T(8,128)}, f32[8,2,96,64]{2,3,1,0:T(8,128)}, u32[]{:S(2)}, u32[]{:S(2)}) %collective-permute-start.12) | collective-permute-done | bytes 393248 | tf_op jit(solution)/shard_map/ppermute | solution.py:63
  459.1 2.2 copy.28
  (77 shorter events, 59.3 us)
Async XLA Ops:
  6.5 99.9 %reduce-scatter.3.cloned.1.call-start = ((), (), s32[]{:S(2)}) async-start(), calls=%async_computation.2 | async-start | bytes 3342336 | tf_op jit(solution)/shard_map/reduce_scatter | solution.py:37
  23.5 144.4 %all-gather.3.cloned.1.call-start = ((), (), s32[]{:S(2)}) async-start(), calls=%async_computation.3 | async-start | bytes 3342336 | tf_op jit(solution)/shard_map/all_gather | solution.py:42
  106.5 4.7 %collective-permute-start = (bf16[4,2,96,128]{3,2,1,0:T(8,128)(2,1)}, bf16[4,2,96,128]{3,2,1,0:T(8,128)(2,1)S(1)}, u32[]{:S(2)}, u32[]{:S(2)}) collective-permute-start(bf16[4,2,96,128]{3,2,1,0:T(8,128)(2,1)} %reduce-scatter.3.cloned.1.call-done), channel_id=1, source_target_pairs={{0,8},{8,0},{1,9},{9,1},{2,10},{10,2},{3,11},{11,3},{4,12},{12,4},... | collective-permute-start | bytes 589832 | tf_op jit(solution)/shard_map/ppermute | solution.py:38
  112.9 176.2 %reduce-scatter.5.cloned.1.call-start = ((), (), s32[]{:S(2)}) async-start(), calls=%async_computation.4 | async-start | bytes 3342336 | tf_op jit(solution)/shard_map/reduce_scatter | solution.py:37
  170.8 2.2 copy-start.3
  180.1 2.6 copy-start
  182.7 6.4 %collective-permute-start.2 = (f32[4,8,2,96,128]{4,3,2,1,0:T(8,128)S(1)}, f32[4,8,2,96,128]{4,3,2,1,0:T(8,128)}, u32[]{:S(2)}, u32[]{:S(2)}) collective-permute-start(f32[4,8,2,96,128]{4,3,2,1,0:T(8,128)S(1)} %dynamic-slice_bitcast_fusion.1), channel_id=1, source_target_pairs={{0,1},{1,0},{2,3},{3,2},{4,5},{5,4},{6,7},{7,6},{8,9},{9,8},{10,11... | collective-permute-start | bytes 9437192 | tf_op jit(solution)/shard_map/ppermute | solution.py:54
  183.7 166.8 %all-gather.5.cloned.1.call-start = ((), (), s32[]{:S(2)}) async-start(), calls=%async_computation.5 | async-start | bytes 3342336 | tf_op jit(solution)/shard_map/all_gather | solution.py:42
  193.7 1.6 copy-start.1
  199.0 32.4 %collective-permute-start.6 = (f32[8,2,96,64]{2,3,1,0:T(8,128)}, f32[8,2,96,64]{2,3,1,0:T(8,128)}, u32[]{:S(2)}, u32[]{:S(2)}) collective-permute-start(f32[8,2,96,64]{2,3,1,0:T(8,128)} %bitcast.113), channel_id=1, source_target_pairs={{0,6},{2,0},{4,2},{6,4},{1,7},{3,1},{5,3},{7,5},{8,14},{10,8},{12,... | collective-permute-start | bytes 1179656 | tf_op jit(solution)/shard_map/ppermute | solution.py:64
  206.5 31.4 %collective-permute-start.3 = (f32[8,2,96,64]{2,3,1,0:T(8,128)}, f32[8,2,96,64]{2,3,1,0:T(8,128)}, u32[]{:S(2)}, u32[]{:S(2)}) collective-permute-start(f32[8,2,96,64]{2,3,1,0:T(8,128)} %bitcast.115), channel_id=1, source_target_pairs={{0,2},{2,4},{4,6},{6,0},{1,3},{3,5},{5,7},{7,1},{8,10},{10,12},{12... | collective-permute-start | bytes 1179656 | tf_op jit(solution)/shard_map/ppermute | solution.py:63
  233.5 17.8 %collective-permute-start.7 = (f32[8,2,96,64]{2,3,1,0:T(8,128)}, f32[8,2,96,64]{2,3,1,0:T(8,128)}, u32[]{:S(2)}, u32[]{:S(2)}) collective-permute-start(f32[8,2,96,64]{2,3,1,0:T(8,128)} %bitcast_add_fusion.11), channel_id=1, source_target_pairs={{0,6},{2,0},{4,2},{6,4},{1,7},{3,1},{5,3},{7,5},{8,14},{10,8},{12,... | collective-permute-start | bytes 1179656 | tf_op jit(solution)/shard_map/ppermute | solution.py:64
  240.0 21.8 %collective-permute-start.4 = (f32[8,2,96,64]{2,3,1,0:T(8,128)}, f32[8,2,96,64]{2,3,1,0:T(8,128)}, u32[]{:S(2)}, u32[]{:S(2)}) collective-permute-start(f32[8,2,96,64]{2,3,1,0:T(8,128)} %bitcast_add_fusion.13), channel_id=1, source_target_pairs={{0,2},{2,4},{4,6},{6,0},{1,3},{3,5},{5,7},{7,1},{8,10},{10,12},{12... | collective-permute-start | bytes 1179656 | tf_op jit(solution)/shard_map/ppermute | solution.py:63
  253.3 22.1 %collective-permute-start.8 = (f32[8,2,96,64]{2,3,1,0:T(8,128)}, f32[8,2,96,64]{2,3,1,0:T(8,128)}, u32[]{:S(2)}, u32[]{:S(2)}) collective-permute-start(f32[8,2,96,64]{2,3,1,0:T(8,128)} %bitcast_add_fusion.10), channel_id=1, source_target_pairs={{0,6},{2,0},{4,2},{6,4},{1,7},{3,1},{5,3},{7,5},{8,14},{10,8},{12,... | collective-permute-start | bytes 1179656 | tf_op jit(solution)/shard_map/ppermute | solution.py:64
  263.9 21.6 %collective-permute-start.5 = (f32[8,2,96,64]{2,3,1,0:T(8,128)}, f32[8,2,96,64]{2,3,1,0:T(8,128)}, u32[]{:S(2)}, u32[]{:S(2)}) collective-permute-start(f32[8,2,96,64]{2,3,1,0:T(8,128)} %bitcast_add_fusion.12), channel_id=1, source_target_pairs={{0,2},{2,4},{4,6},{6,0},{1,3},{3,5},{5,7},{7,1},{8,10},{10,12},{12... | collective-permute-start | bytes 1179656 | tf_op jit(solution)/shard_map/ppermute | solution.py:63
  289.1 4.8 %copy-start.6 = (bf16[4,2,96,128]{3,2,1,0:T(8,128)(2,1)S(1)}, bf16[4,2,96,128]{3,2,1,0:T(8,128)(2,1)}, u32[]{:S(2)}) copy-start(bf16[4,2,96,128]{3,2,1,0:T(8,128)(2,1)} %reduce-scatter.5.cloned.1.call-done) | copy-start | bytes 589828
  289.2 4.8 %collective-permute-start.1 = (bf16[4,2,96,128]{3,2,1,0:T(8,128)(2,1)}, bf16[4,2,96,128]{3,2,1,0:T(8,128)(2,1)S(1)}, u32[]{:S(2)}, u32[]{:S(2)}) collective-permute-start(bf16[4,2,96,128]{3,2,1,0:T(8,128)(2,1)} %reduce-scatter.5.cloned.1.call-done), channel_id=1, source_target_pairs={{0,8},{8,0},{1,9},{9,1},{2,10},{10,2},{3,11},{11,3},{4,12},{12,4},... | collective-permute-start | bytes 589832 | tf_op jit(solution)/shard_map/ppermute | solution.py:38
  353.4 2.2 copy-start.4
  357.8 6.4 %collective-permute-start.9 = (f32[4,8,2,96,128]{4,3,2,1,0:T(8,128)S(1)}, f32[4,8,2,96,128]{4,3,2,1,0:T(8,128)S(1)}, u32[]{:S(2)}, u32[]{:S(2)}) collective-permute-start(f32[4,8,2,96,128]{4,3,2,1,0:T(8,128)S(1)} %dynamic-slice_bitcast_fusion), channel_id=1, source_target_pairs={{0,1},{1,0},{2,3},{3,2},{4,5},{5,4},{6,7},{7,6},{8,9},{9,8},{10,11... | collective-permute-start | bytes 9437192 | tf_op jit(solution)/shard_map/ppermute | solution.py:54
  365.9 1.6 copy-start.2
  371.2 32.4 %collective-permute-start.13 = (f32[8,2,96,64]{2,3,1,0:T(8,128)}, f32[8,2,96,64]{2,3,1,0:T(8,128)}, u32[]{:S(2)}, u32[]{:S(2)}) collective-permute-start(f32[8,2,96,64]{2,3,1,0:T(8,128)} %bitcast.114), channel_id=1, source_target_pairs={{0,6},{2,0},{4,2},{6,4},{1,7},{3,1},{5,3},{7,5},{8,14},{10,8},{12,... | collective-permute-start | bytes 1179656 | tf_op jit(solution)/shard_map/ppermute | solution.py:64
  378.7 33.8 %collective-permute-start.10 = (f32[8,2,96,64]{2,3,1,0:T(8,128)}, f32[8,2,96,64]{2,3,1,0:T(8,128)}, u32[]{:S(2)}, u32[]{:S(2)}) collective-permute-start(f32[8,2,96,64]{2,3,1,0:T(8,128)} %bitcast.116), channel_id=1, source_target_pairs={{0,2},{2,4},{4,6},{6,0},{1,3},{3,5},{5,7},{7,1},{8,10},{10,12},{12... | collective-permute-start | bytes 1179656 | tf_op jit(solution)/shard_map/ppermute | solution.py:63
  405.7 17.7 %collective-permute-start.14 = (f32[8,2,96,64]{2,3,1,0:T(8,128)}, f32[8,2,96,64]{2,3,1,0:T(8,128)}, u32[]{:S(2)}, u32[]{:S(2)}) collective-permute-start(f32[8,2,96,64]{2,3,1,0:T(8,128)} %bitcast_add_fusion.7), channel_id=1, source_target_pairs={{0,6},{2,0},{4,2},{6,4},{1,7},{3,1},{5,3},{7,5},{8,14},{10,8},{12,... | collective-permute-start | bytes 1179656 | tf_op jit(solution)/shard_map/ppermute | solution.py:64
  414.5 19.5 %collective-permute-start.11 = (f32[8,2,96,64]{2,3,1,0:T(8,128)}, f32[8,2,96,64]{2,3,1,0:T(8,128)}, u32[]{:S(2)}, u32[]{:S(2)}) collective-permute-start(f32[8,2,96,64]{2,3,1,0:T(8,128)} %bitcast_add_fusion.9), channel_id=1, source_target_pairs={{0,2},{2,4},{4,6},{6,0},{1,3},{3,5},{5,7},{7,1},{8,10},{10,12},{12... | collective-permute-start | bytes 1179656 | tf_op jit(solution)/shard_map/ppermute | solution.py:63
  424.7 22.9 %collective-permute-start.15 = (f32[8,2,96,64]{2,3,1,0:T(8,128)S(1)}, f32[8,2,96,64]{2,3,1,0:T(8,128)}, u32[]{:S(2)}, u32[]{:S(2)}) collective-permute-start(f32[8,2,96,64]{2,3,1,0:T(8,128)S(1)} %bitcast_add_fusion.6), channel_id=1, source_target_pairs={{0,6},{2,0},{4,2},{6,4},{1,7},{3,1},{5,3},{7,5},{8,14},{10,8},{12,... | collective-permute-start | bytes 1179656 | tf_op jit(solution)/shard_map/ppermute | solution.py:64
  436.1 26.4 %copy-start.5 = (bf16[8,2,96,128]{3,2,1,0:T(8,128)(2,1)S(1)}, bf16[8,2,96,128]{3,2,1,0:T(8,128)(2,1)}, u32[]{:S(2)}) copy-start(bf16[8,2,96,128]{3,2,1,0:T(8,128)(2,1)} %pad_maximum_fusion) | copy-start | bytes 1179652
  436.1 23.0 %collective-permute-start.12 = (f32[8,2,96,64]{2,3,1,0:T(8,128)}, f32[8,2,96,64]{2,3,1,0:T(8,128)}, u32[]{:S(2)}, u32[]{:S(2)}) collective-permute-start(f32[8,2,96,64]{2,3,1,0:T(8,128)} %bitcast_add_fusion.8), channel_id=1, source_target_pairs={{0,2},{2,4},{4,6},{6,0},{1,3},{3,5},{5,7},{7,1},{8,10},{10,12},{12... | collective-permute-start | bytes 1179656 | tf_op jit(solution)/shard_map/ppermute | solution.py:63
Sparse Core Ops, SparseCore 0:
  23.6 82.8 reduce-scatter.2
  113.0 54.7 all-gather.2
  183.8 77.8 reduce-scatter.4
  294.9 55.5 all-gather.4
where the time goes:
time: 473 us; the launch traced here: 471 us
  waiting for transfers between devices  310 us (66%)
  local copies, waits for them, and re-layouts  58.1 us (12%)
  other arithmetic  50.2 us (11%)
  starting transfers between devices  29.8 us (6%)
  between operations  13.4 us (3%)
  matrix products  9.62 us (2%)
    all_gather x2, waiting for transfers between devices, broadcast(): return (lax.all_gather(part, PLANE, axis=0, tiled=True), pending)  110 us
    reduce_scatter x2, waiting for transfers between devices, broadcast(): part = lax.psum_scatter(piece, PLANE, scatter_dimension=0, tiled=True)  83 us
    ppermute x6, waiting for transfers between devices, shot_reduce(): got_b = lax.ppermute(acc_b, 'zh', perm=down)  73.4 us
    ppermute x6, waiting for transfers between devices, shot_reduce(): got_f = lax.ppermute(acc_f, 'zh', perm=up)  27.4 us
    ppermute x6, starting transfers between devices, shot_reduce(): got_b = lax.ppermute(acc_b, 'zh', perm=down)  22 us
    dynamic_slice x6, local copies, waits for them, and re-layouts, shot_reduce(): lax.dynamic_index_in_dim(forward, (zh - 2 - step) % nz, axis=0, keepdims=...  11.7 us
    dynamic_slice x6, local copies, waits for them, and re-layouts, shot_reduce(): lax.dynamic_index_in_dim(backward, (zh + 2 + step) % nz, axis=0, keepdims...  11.7 us
    ppermute x2, waiting for transfers between devices, shot_reduce(): mine = keep + lax.ppermute(send, 'c', perm=[(0, 1), (1, 0)])  10.6 us
  transfers between devices with their start and end apart: 20, of which 17 were waited for; matrix products, arithmetic and copies ran while one was open for 13% of the time, Pallas kernels for 0%

commit v1 on v0

--- a/solution.py
+++ b/solution.py
@@ -9,6 +9,18 @@
 WINDOWS = 8
 CHUNKS = 2
 PLANE = ("y", "x")
+
+
+def produce_case(sheet):
+    return jnp.concatenate(
+        jax.lax.all_to_all(
+            jnp.stack([sheet] * jax.lax.axis_size(PLANE)),
+            axis_name=PLANE,
+            split_axis=0,
+            concat_axis=0,
+        ),
+        axis=0,
+    )
 
 
 def taper_weights(taper_windows):
@@ -39,7 +51,7 @@
     part = part + other
     if pending is not None:
         part, pending = lax.optimization_barrier((part, pending))
-    return (lax.all_gather(part, PLANE, axis=0, tiled=True), pending)
+    return (produce_case(part), pending)
 
 
 def shot_reduce(partial):

time: 473 us -> 450 us (0.951)
  the two profiles are of different devices: /device:TPU:1 before, /device:TPU:2 now
where the time goes in v1:
time: 450 us; the launch traced here: 449 us
  waiting for transfers between devices  235 us (52%)
  local copies, waits for them, and re-layouts  63 us (14%)
  other arithmetic  45.2 us (10%)
  blocking collectives  42.4 us (9%)
  starting transfers between devices  40.2 us (9%)
  between operations  13.8 us (3%)
  matrix products  9.62 us (2%)
    reduce_scatter x2, waiting for transfers between devices, broadcast(): part = lax.psum_scatter(piece, PLANE, scatter_dimension=0, tiled=True)  83.6 us
    ppermute x6, waiting for transfers between devices, shot_reduce(): got_b = lax.ppermute(acc_b, 'zh', perm=down)  80.2 us
    all_to_all x1, blocking collectives, produce_case(): jax.lax.all_to_all(jnp.stack([sheet] * jax.lax.axis_size(PLANE)), axis_na...  42.4 us
    all_to_all x1, waiting for transfers between devices, produce_case(): jax.lax.all_to_all(jnp.stack([sheet] * jax.lax.axis_size(PLANE)), axis_na...  35.3 us
    ppermute x6, starting transfers between devices, shot_reduce(): got_b = lax.ppermute(acc_b, 'zh', perm=down)  31.8 us
    ppermute x6, waiting for transfers between devices, shot_reduce(): got_f = lax.ppermute(acc_f, 'zh', perm=up)  16.2 us
    dynamic_slice x6, local copies, waits for them, and re-layouts, shot_reduce(): lax.dynamic_index_in_dim(forward, (zh - 2 - step) % nz, axis=0, keepdims=...  11.8 us
    dynamic_slice x6, local copies, waits for them, and re-layouts, shot_reduce(): lax.dynamic_index_in_dim(backward, (zh + 2 + step) % nz, axis=0, keepdims...  11.8 us
  transfers between devices with their start and end apart: 19, of which 15 were waited for; matrix products, arithmetic and copies ran while one was open for 14% of the time, Pallas kernels for 0%

profile of v1, /device:TPU:2, one launch (start us, length us, event | category | flops | bytes accessed | tf_op | source)
XLA Modules:
  0.0 448.8 jit_solution(8970960231975941722)
XLA Ops:
  7.9 3.7 fusion.28
  11.7 3.8 compare_reduce_fusion
  15.6 4.0 convert_bitcast_fusion
  19.6 3.9 slice_bitcast_fusion
  23.5 83.6 %reduce-scatter.3.cloned.1.call-done = bf16[4,2,96,128]{3,2,1,0:T(8,128)(2,1)} async-done(((bf16[64,2,96,128]{3,2,1,0:T(8,128)(2,1)}), bf16[4,2,96,128]{3,2,1,0:T(8,128)(2,1)}) %reduce-scatter.3.cloned.1.call-update) | async-done | bytes 196624 | tf_op jit(solution)/shard_map/reduce_scatter | solution.py:49
  108.6 4.3 collective-permute-done
  114.0 2.3 stack.16
  116.3 5.7 %all-to-all-start = ((bf16[16,4,2,96,128]{4,3,1,2,0:T(8,128)(2,1)}), bf16[16,4,2,96,128]{4,3,1,2,0:T(8,128)(2,1)S(1)}, u32[]{:S(2)}, u32[]{:S(2)}) async-start(bf16[16,4,2,96,128]{4,3,1,2,0:T(8,128)(2,1)} %stack.16), calls=%async_computation.1 | async-start | bytes 6291456 | tf_op jit(solution)/shard_map/all_to_all | solution.py:16
  122.8 35.3 %all-to-all-done = bf16[16,4,2,96,128]{4,3,1,2,0:T(8,128)(2,1)S(1)} async-done(((bf16[16,4,2,96,128]{4,3,1,2,0:T(8,128)(2,1)}), bf16[16,4,2,96,128]{4,3,1,2,0:T(8,128)(2,1)S(1)}, u32[]{:S(2)}, u32[]{:S(2)}) %all-to-all-start) | async-done | bytes 3145760 | tf_op jit(solution)/shard_map/all_to_all | solution.py:16
  162.3 3.6 fusion
  165.9 3.4 broadcast_multiply_fusion.1
  169.6 2.4 copy-done
  172.1 5.7 %collective-permute-done.2 = f32[4,8,2,96,128]{4,3,2,1,0:T(8,128)} collective-permute-done((f32[4,8,2,96,128]{4,3,2,1,0:T(8,128)S(1)}, f32[4,8,2,96,128]{4,3,2,1,0:T(8,128)}, u32[]{:S(2)}, u32[]{:S(2)}) %collective-permute-start.2) | collective-permute-done | bytes 3145760 | tf_op jit(solution)/shard_map/ppermute | solution.py:66
  177.8 3.4 bitcast_add_fusion.1
  185.5 2.2 copy.20
  187.7 4.1 collective-permute-start.6
  193.3 2.2 copy.16
  195.5 2.2 copy.21
  197.7 2.2 copy.17
  199.9 20.6 %collective-permute-done.6 = f32[8,2,96,64]{2,3,1,0:T(8,128)} collective-permute-done((f32[8,2,96,64]{2,3,1,0:T(8,128)}, f32[8,2,96,64]{2,3,1,0:T(8,128)}, u32[]{:S(2)}, u32[]{:S(2)}) %collective-permute-start.6) | collective-permute-done | bytes 393248 | tf_op jit(solution)/shard_map/ppermute | solution.py:76
  222.5 4.7 %collective-permute-start.7 = (f32[8,2,96,64]{2,3,1,0:T(8,128)}, f32[8,2,96,64]{2,3,1,0:T(8,128)}, u32[]{:S(2)}, u32[]{:S(2)}) collective-permute-start(f32[8,2,96,64]{2,3,1,0:T(8,128)} %bitcast_add_fusion.11), channel_id=1, source_target_pairs={{0,6},{2,0},{4,2},{6,4},{1,7},{3,1},{5,3},{7,5},{8,14},{10,8},{12,... | collective-permute-start | bytes 1179656 | tf_op jit(solution)/shard_map/ppermute | solution.py:76
  229.2 2.2 copy.22
  231.4 2.2 copy.18
  233.7 6.4 %collective-permute-done.7 = f32[8,2,96,64]{2,3,1,0:T(8,128)} collective-permute-done((f32[8,2,96,64]{2,3,1,0:T(8,128)}, f32[8,2,96,64]{2,3,1,0:T(8,128)}, u32[]{:S(2)}, u32[]{:S(2)}) %collective-permute-start.7) | collective-permute-done | bytes 393248 | tf_op jit(solution)/shard_map/ppermute | solution.py:76
  242.1 10.4 %collective-permute-start.8 = (f32[8,2,96,64]{2,3,1,0:T(8,128)}, f32[8,2,96,64]{2,3,1,0:T(8,128)}, u32[]{:S(2)}, u32[]{:S(2)}) collective-permute-start(f32[8,2,96,64]{2,3,1,0:T(8,128)} %bitcast_add_fusion.10), channel_id=1, source_target_pairs={{0,6},{2,0},{4,2},{6,4},{1,7},{3,1},{5,3},{7,5},{8,14},{10,8},{12,... | collective-permute-start | bytes 1179656 | tf_op jit(solution)/shard_map/ppermute | solution.py:76
  255.2 9.0 %collective-permute-done.8 = f32[8,2,96,64]{2,3,1,0:T(8,128)} collective-permute-done((f32[8,2,96,64]{2,3,1,0:T(8,128)}, f32[8,2,96,64]{2,3,1,0:T(8,128)}, u32[]{:S(2)}, u32[]{:S(2)}) %collective-permute-start.8) | collective-permute-done | bytes 393248 | tf_op jit(solution)/shard_map/ppermute | solution.py:76
  264.2 2.2 copy.23
  266.4 9.8 %collective-permute-done.5 = f32[8,2,96,64]{2,3,1,0:T(8,128)} collective-permute-done((f32[8,2,96,64]{2,3,1,0:T(8,128)}, f32[8,2,96,64]{2,3,1,0:T(8,128)}, u32[]{:S(2)}, u32[]{:S(2)}) %collective-permute-start.5) | collective-permute-done | bytes 393248 | tf_op jit(solution)/shard_map/ppermute | solution.py:75
  276.2 2.2 copy.19
  282.2 3.6 collective-permute-done.1
  286.7 42.4 %all_to_all.10 = bf16[16,4,2,96,128]{4,3,1,2,0:T(8,128)(2,1)S(1)} all-to-all(bf16[16,4,2,96,128]{4,3,1,2,0:T(8,128)(2,1)S(1)} %stack.20), channel_id=1, replica_groups=mesh['y'=4,'x'=4,'zl'=2,'zh'=4,'c'=2] {'y','x'}, dimensions={0} | all-to-all | bytes 6291456 | tf_op jit(solution)/shard_map/all_to_all | solution.py:16
  335.7 5.6 %collective-permute-done.9 = f32[4,8,2,96,128]{4,3,2,1,0:T(8,128)S(1)} collective-permute-done((f32[4,8,2,96,128]{4,3,2,1,0:T(8,128)S(1)}, f32[4,8,2,96,128]{4,3,2,1,0:T(8,128)S(1)}, u32[]{:S(2)}, u32[]{:S(2)}) %collective-permute-start.9) | collective-permute-done | bytes 3145760 | tf_op jit(solution)/shard_map/ppermute | solution.py:66
  346.2 2.2 copy.31
  348.4 4.3 collective-permute-start.13
  356.4 2.2 copy.32
  358.6 15.8 %collective-permute-done.13 = f32[8,2,96,64]{2,3,1,0:T(8,128)} collective-permute-done((f32[8,2,96,64]{2,3,1,0:T(8,128)}, f32[8,2,96,64]{2,3,1,0:T(8,128)}, u32[]{:S(2)}, u32[]{:S(2)}) %collective-permute-start.13) | collective-permute-done | bytes 393248 | tf_op jit(solution)/shard_map/ppermute | solution.py:76
  376.5 3.7 collective-permute-start.14
  380.2 2.2 copy.28
  384.6 2.2 copy.33
  386.8 2.2 copy.29
  389.0 14.2 %collective-permute-done.14 = f32[8,2,96,64]{2,3,1,0:T(8,128)} collective-permute-done((f32[8,2,96,64]{2,3,1,0:T(8,128)}, f32[8,2,96,64]{2,3,1,0:T(8,128)}, u32[]{:S(2)}, u32[]{:S(2)}) %collective-permute-start.14) | collective-permute-done | bytes 393248 | tf_op jit(solution)/shard_map/ppermute | solution.py:76
  404.4 4.7 %collective-permute-start.15 = (f32[8,2,96,64]{2,3,1,0:T(8,128)S(1)}, f32[8,2,96,64]{2,3,1,0:T(8,128)}, u32[]{:S(2)}, u32[]{:S(2)}) collective-permute-start(f32[8,2,96,64]{2,3,1,0:T(8,128)S(1)} %bitcast_add_fusion.6), channel_id=1, source_target_pairs={{0,6},{2,0},{4,2},{6,4},{1,7},{3,1},{5,3},{7,5},{8,14},{10,8},{12,... | collective-permute-start | bytes 1179656 | tf_op jit(solution)/shard_map/ppermute | solution.py:76
  409.1 2.5 collective-permute-done.11
  413.6 14.4 %collective-permute-done.15 = f32[8,2,96,64]{2,3,1,0:T(8,128)} collective-permute-done((f32[8,2,96,64]{2,3,1,0:T(8,128)S(1)}, f32[8,2,96,64]{2,3,1,0:T(8,128)}, u32[]{:S(2)}, u32[]{:S(2)}) %collective-permute-start.15) | collective-permute-done | bytes 393248 | tf_op jit(solution)/shard_map/ppermute | solution.py:76
  428.0 2.2 copy.34
  430.2 2.2 fusion.14
  432.4 3.9 collective-permute-done.12
  436.3 2.2 copy.30
  (80 shorter events, 54.6 us)
Async XLA Ops:
  6.5 100.5 %reduce-scatter.3.cloned.1.call-start = ((), (), s32[]{:S(2)}) async-start(), calls=%async_computation.4 | async-start | bytes 3342336 | tf_op jit(solution)/shard_map/reduce_scatter | solution.py:49
  107.1 5.9 %collective-permute-start = (bf16[4,2,96,128]{3,2,1,0:T(8,128)(2,1)}, bf16[4,2,96,128]{3,2,1,0:T(8,128)(2,1)S(1)}, u32[]{:S(2)}, u32[]{:S(2)}) collective-permute-start(bf16[4,2,96,128]{3,2,1,0:T(8,128)(2,1)} %reduce-scatter.3.cloned.1.call-done), channel_id=1, source_target_pairs={{0,8},{8,0},{1,9},{9,1},{2,10},{10,2},{3,11},{11,3},{4,12},{12,4},... | collective-permute-start | bytes 589832 | tf_op jit(solution)/shard_map/ppermute | solution.py:50
  116.3 41.8 %all-to-all-start = ((bf16[16,4,2,96,128]{4,3,1,2,0:T(8,128)(2,1)}), bf16[16,4,2,96,128]{4,3,1,2,0:T(8,128)(2,1)S(1)}, u32[]{:S(2)}, u32[]{:S(2)}) async-start(bf16[16,4,2,96,128]{4,3,1,2,0:T(8,128)(2,1)} %stack.16), calls=%async_computation.1 | async-start | bytes 6291456 | tf_op jit(solution)/shard_map/all_to_all | solution.py:16
  122.0 157.9 %reduce-scatter.5.cloned.1.call-start = ((), (), s32[]{:S(2)}) async-start(), calls=%async_computation.5 | async-start | bytes 3342336 | tf_op jit(solution)/shard_map/reduce_scatter | solution.py:49
  160.1 2.2 copy-start.3
  169.4 2.6 copy-start
  172.0 5.8 %collective-permute-start.2 = (f32[4,8,2,96,128]{4,3,2,1,0:T(8,128)S(1)}, f32[4,8,2,96,128]{4,3,2,1,0:T(8,128)}, u32[]{:S(2)}, u32[]{:S(2)}) collective-permute-start(f32[4,8,2,96,128]{4,3,2,1,0:T(8,128)S(1)} %dynamic-slice_bitcast_fusion.1), channel_id=1, source_target_pairs={{0,1},{1,0},{2,3},{3,2},{4,5},{5,4},{6,7},{7,6},{8,9},{9,8},{10,11... | collective-permute-start | bytes 9437192 | tf_op jit(solution)/shard_map/ppermute | solution.py:66
  182.4 1.6 copy-start.1
  187.7 32.8 %collective-permute-start.6 = (f32[8,2,96,64]{2,3,1,0:T(8,128)}, f32[8,2,96,64]{2,3,1,0:T(8,128)}, u32[]{:S(2)}, u32[]{:S(2)}) collective-permute-start(f32[8,2,96,64]{2,3,1,0:T(8,128)} %bitcast.117), channel_id=1, source_target_pairs={{0,6},{2,0},{4,2},{6,4},{1,7},{3,1},{5,3},{7,5},{8,14},{10,8},{12,... | collective-permute-start | bytes 1179656 | tf_op jit(solution)/shard_map/ppermute | solution.py:76
  195.5 31.7 %collective-permute-start.3 = (f32[8,2,96,64]{2,3,1,0:T(8,128)}, f32[8,2,96,64]{2,3,1,0:T(8,128)}, u32[]{:S(2)}, u32[]{:S(2)}) collective-permute-start(f32[8,2,96,64]{2,3,1,0:T(8,128)} %bitcast.119), channel_id=1, source_target_pairs={{0,2},{2,4},{4,6},{6,0},{1,3},{3,5},{5,7},{7,1},{8,10},{10,12},{12... | collective-permute-start | bytes 1179656 | tf_op jit(solution)/shard_map/ppermute | solution.py:75
  222.5 17.5 %collective-permute-start.7 = (f32[8,2,96,64]{2,3,1,0:T(8,128)}, f32[8,2,96,64]{2,3,1,0:T(8,128)}, u32[]{:S(2)}, u32[]{:S(2)}) collective-permute-start(f32[8,2,96,64]{2,3,1,0:T(8,128)} %bitcast_add_fusion.11), channel_id=1, source_target_pairs={{0,6},{2,0},{4,2},{6,4},{1,7},{3,1},{5,3},{7,5},{8,14},{10,8},{12,... | collective-permute-start | bytes 1179656 | tf_op jit(solution)/shard_map/ppermute | solution.py:76
  229.2 23.3 %collective-permute-start.4 = (f32[8,2,96,64]{2,3,1,0:T(8,128)}, f32[8,2,96,64]{2,3,1,0:T(8,128)}, u32[]{:S(2)}, u32[]{:S(2)}) collective-permute-start(f32[8,2,96,64]{2,3,1,0:T(8,128)} %bitcast_add_fusion.13), channel_id=1, source_target_pairs={{0,2},{2,4},{4,6},{6,0},{1,3},{3,5},{5,7},{7,1},{8,10},{10,12},{12... | collective-permute-start | bytes 1179656 | tf_op jit(solution)/shard_map/ppermute | solution.py:75
  242.1 22.1 %collective-permute-start.8 = (f32[8,2,96,64]{2,3,1,0:T(8,128)}, f32[8,2,96,64]{2,3,1,0:T(8,128)}, u32[]{:S(2)}, u32[]{:S(2)}) collective-permute-start(f32[8,2,96,64]{2,3,1,0:T(8,128)} %bitcast_add_fusion.10), channel_id=1, source_target_pairs={{0,6},{2,0},{4,2},{6,4},{1,7},{3,1},{5,3},{7,5},{8,14},{10,8},{12,... | collective-permute-start | bytes 1179656 | tf_op jit(solution)/shard_map/ppermute | solution.py:76
  254.6 21.6 %collective-permute-start.5 = (f32[8,2,96,64]{2,3,1,0:T(8,128)}, f32[8,2,96,64]{2,3,1,0:T(8,128)}, u32[]{:S(2)}, u32[]{:S(2)}) collective-permute-start(f32[8,2,96,64]{2,3,1,0:T(8,128)} %bitcast_add_fusion.12), channel_id=1, source_target_pairs={{0,2},{2,4},{4,6},{6,0},{1,3},{3,5},{5,7},{7,1},{8,10},{10,12},{12... | collective-permute-start | bytes 1179656 | tf_op jit(solution)/shard_map/ppermute | solution.py:75
  279.9 6.0 %copy-start.6 = (bf16[4,2,96,128]{3,2,1,0:T(8,128)(2,1)S(1)}, bf16[4,2,96,128]{3,2,1,0:T(8,128)(2,1)}, u32[]{:S(2)}) copy-start(bf16[4,2,96,128]{3,2,1,0:T(8,128)(2,1)} %reduce-scatter.5.cloned.1.call-done) | copy-start | bytes 589828
  279.9 6.0 %collective-permute-start.1 = (bf16[4,2,96,128]{3,2,1,0:T(8,128)(2,1)}, bf16[4,2,96,128]{3,2,1,0:T(8,128)(2,1)S(1)}, u32[]{:S(2)}, u32[]{:S(2)}) collective-permute-start(bf16[4,2,96,128]{3,2,1,0:T(8,128)(2,1)} %reduce-scatter.5.cloned.1.call-done), channel_id=1, source_target_pairs={{0,8},{8,0},{1,9},{9,1},{2,10},{10,2},{3,11},{11,3},{4,12},{12,4},... | collective-permute-start | bytes 589832 | tf_op jit(solution)/shard_map/ppermute | solution.py:50
  331.0 2.2 copy-start.4
  335.4 6.0 %collective-permute-start.9 = (f32[4,8,2,96,128]{4,3,2,1,0:T(8,128)S(1)}, f32[4,8,2,96,128]{4,3,2,1,0:T(8,128)S(1)}, u32[]{:S(2)}, u32[]{:S(2)}) collective-permute-start(f32[4,8,2,96,128]{4,3,2,1,0:T(8,128)S(1)} %dynamic-slice_bitcast_fusion), channel_id=1, source_target_pairs={{0,1},{1,0},{2,3},{3,2},{4,5},{5,4},{6,7},{7,6},{8,9},{9,8},{10,11... | collective-permute-start | bytes 9437192 | tf_op jit(solution)/shard_map/ppermute | solution.py:66
  343.1 1.6 copy-start.2
  348.4 25.9 %collective-permute-start.13 = (f32[8,2,96,64]{2,3,1,0:T(8,128)}, f32[8,2,96,64]{2,3,1,0:T(8,128)}, u32[]{:S(2)}, u32[]{:S(2)}) collective-permute-start(f32[8,2,96,64]{2,3,1,0:T(8,128)} %bitcast.118), channel_id=1, source_target_pairs={{0,6},{2,0},{4,2},{6,4},{1,7},{3,1},{5,3},{7,5},{8,14},{10,8},{12,... | collective-permute-start | bytes 1179656 | tf_op jit(solution)/shard_map/ppermute | solution.py:76
  356.4 26.0 %collective-permute-start.10 = (f32[8,2,96,64]{2,3,1,0:T(8,128)}, f32[8,2,96,64]{2,3,1,0:T(8,128)}, u32[]{:S(2)}, u32[]{:S(2)}) collective-permute-start(f32[8,2,96,64]{2,3,1,0:T(8,128)} %bitcast.120), channel_id=1, source_target_pairs={{0,2},{2,4},{4,6},{6,0},{1,3},{3,5},{5,7},{7,1},{8,10},{10,12},{12... | collective-permute-start | bytes 1179656 | tf_op jit(solution)/shard_map/ppermute | solution.py:75
  376.5 26.7 %collective-permute-start.14 = (f32[8,2,96,64]{2,3,1,0:T(8,128)}, f32[8,2,96,64]{2,3,1,0:T(8,128)}, u32[]{:S(2)}, u32[]{:S(2)}) collective-permute-start(f32[8,2,96,64]{2,3,1,0:T(8,128)} %bitcast_add_fusion.7), channel_id=1, source_target_pairs={{0,6},{2,0},{4,2},{6,4},{1,7},{3,1},{5,3},{7,5},{8,14},{10,8},{12,... | collective-permute-start | bytes 1179656 | tf_op jit(solution)/shard_map/ppermute | solution.py:76
  384.5 27.1 %collective-permute-start.11 = (f32[8,2,96,64]{2,3,1,0:T(8,128)}, f32[8,2,96,64]{2,3,1,0:T(8,128)}, u32[]{:S(2)}, u32[]{:S(2)}) collective-permute-start(f32[8,2,96,64]{2,3,1,0:T(8,128)} %bitcast_add_fusion.9), channel_id=1, source_target_pairs={{0,2},{2,4},{4,6},{6,0},{1,3},{3,5},{5,7},{7,1},{8,10},{10,12},{12... | collective-permute-start | bytes 1179656 | tf_op jit(solution)/shard_map/ppermute | solution.py:75
  404.4 23.6 %collective-permute-start.15 = (f32[8,2,96,64]{2,3,1,0:T(8,128)S(1)}, f32[8,2,96,64]{2,3,1,0:T(8,128)}, u32[]{:S(2)}, u32[]{:S(2)}) collective-permute-start(f32[8,2,96,64]{2,3,1,0:T(8,128)S(1)} %bitcast_add_fusion.6), channel_id=1, source_target_pairs={{0,6},{2,0},{4,2},{6,4},{1,7},{3,1},{5,3},{7,5},{8,14},{10,8},{12,... | collective-permute-start | bytes 1179656 | tf_op jit(solution)/shard_map/ppermute | solution.py:76
  413.6 26.1 %copy-start.5 = (bf16[8,2,96,128]{3,2,1,0:T(8,128)(2,1)S(1)}, bf16[8,2,96,128]{3,2,1,0:T(8,128)(2,1)}, u32[]{:S(2)}) copy-start(bf16[8,2,96,128]{3,2,1,0:T(8,128)(2,1)} %pad_maximum_fusion) | copy-start | bytes 1179652
  413.6 22.6 %collective-permute-start.12 = (f32[8,2,96,64]{2,3,1,0:T(8,128)}, f32[8,2,96,64]{2,3,1,0:T(8,128)}, u32[]{:S(2)}, u32[]{:S(2)}) collective-permute-start(f32[8,2,96,64]{2,3,1,0:T(8,128)} %bitcast_add_fusion.8), channel_id=1, source_target_pairs={{0,2},{2,4},{4,6},{6,0},{1,3},{3,5},{5,7},{7,1},{8,10},{10,12},{12... | collective-permute-start | bytes 1179656 | tf_op jit(solution)/shard_map/ppermute | solution.py:75
Sparse Core Ops, SparseCore 0:
  23.6 83.4 reduce-scatter.2
  172.2 81.7 reduce-scatter.4
